TPU v7x, 256 devices: a whole 4x4x8 slice. The times are simulated.
256 devices in a mesh: pos: 64 (over x, y_hi, z), section: 4 (over y_lo, core).
Axes of the slice: x: 4, y: 4 (y_hi: 2, y_lo: 2; y = y_hi * 2 + y_lo), z: 8, core: 2. Of those that a mesh axis runs over, the one named last changes fastest.
Arguments:
- sequence_features: bfloat16 [262144, 128], P('pos'), may hold values from -6 to 6
- norm_gain: float32 [4, 2, 128], P('section'), may hold values from 0.5 to 2
- conv_weight: bfloat16 [4, 2, 3, 128, 128], P('section'), may hold values from -0.3125 to 0.3125
- conv_bias: float32 [4, 2, 128], P('section'), may hold values from -3 to 3
- mix_weight: bfloat16 [4, 2, 128, 128], P('section'), may hold values from -0.5 to 0.5
Outputs:
- section_outputs: bfloat16 [4, 262144, 128], P('section', 'pos')
All inputs are finite; a program needn't handle non-finite values.
Results may differ from a plain program's by a relative error of at most 0.024.
Values may be sent and summed in bfloat16 or wider, within the bound.
No kernel may reach another device: no remote copies, remote signals or barrier semaphores. Data moves between devices by JAX's collectives and lax.ppermute only.
A program may use at most 64 MiB of HBM per device.

v0:
```python
import jax
import jax.numpy as jnp
from jax import lax
from jax.sharding import PartitionSpec as P

REDUNDANT = 5


def shifted(block, shift):
    count = lax.axis_size("pos")
    return lax.ppermute(block, "pos", [(i, (i + shift) % count) for i in range(count)])


def prepare(x, gain):
    r = x.astype(jnp.float32)
    meansq = jnp.mean(r * r, axis=-1, keepdims=True)
    return jax.nn.gelu(r * lax.rsqrt(meansq + 1e-06) * gain, approximate=False).astype(jnp.bfloat16)


def mix(x, before, h, after, taps, bias, mixing):
    conv = jnp.dot(h, taps[1], preferred_element_type=jnp.float32)
    conv = conv + jnp.dot(before, taps[0], preferred_element_type=jnp.float32)
    conv = conv + jnp.dot(after, taps[2], preferred_element_type=jnp.float32)
    g = jax.nn.gelu(conv + bias, approximate=False).astype(jnp.bfloat16)
    return (x.astype(jnp.float32) + jnp.dot(g, mixing, preferred_element_type=jnp.float32)).astype(
        jnp.bfloat16
    )


def widened_layer(x, gain, taps, bias, mixing, shift):
    count = x.shape[0]
    h = prepare(x, gain)
    return mix(
        x[shift : count - shift],
        h[: count - 2 * shift],
        h[shift : count - shift],
        h[2 * shift :],
        taps,
        bias,
        mixing,
    )


def exchanged_layer(x, gain, taps, bias, mixing, shift):
    chunk = x.shape[0]
    h = prepare(x, gain)
    if shift % chunk == 0:
        before = shifted(h, shift // chunk)
        after = shifted(h, -(shift // chunk))
    else:
        before = jnp.concatenate([shifted(h[chunk - shift :], 1), h[: chunk - shift]], axis=0)
        after = jnp.concatenate([h[shift:], shifted(h[:shift], -1)], axis=0)
    return mix(x, before, h, after, taps, bias, mixing)


def body(sequence_features, norm_gain, conv_weight, conv_bias, mix_weight):
    n_section = lax.axis_size("section")
    my_section = lax.axis_index("section")
    per_section = conv_weight.shape[1]
    block, channels = sequence_features.shape
    first_dilation = block // 2 ** (per_section * n_section - 1)
    group = first_dilation // n_section
    runs = block // first_dilation
    matrices = jnp.concatenate(
        [
            conv_weight.reshape(1, per_section * 3, channels, channels),
            mix_weight.reshape(1, per_section, channels, channels),
        ],
        axis=1,
    )
    vectors = jnp.concatenate([norm_gain, conv_bias], axis=1)
    matrices = lax.all_gather(matrices, "section", tiled=True)
    vectors = lax.all_gather(vectors, "section", tiled=True)
    runs_of = sequence_features.reshape(runs, n_section, group, channels)
    x = lax.dynamic_index_in_dim(runs_of, my_section, axis=1, keepdims=False).reshape(
        runs * group, channels
    )
    chunk = x.shape[0]
    shifts = [first_dilation * 2**index // n_section for index in range(per_section * n_section)]
    widen = sum(shifts[:REDUNDANT])
    assert widen <= chunk
    x = jnp.concatenate([shifted(x[chunk - widen :], 1), x, shifted(x[:widen], -1)], axis=0)
    result = None
    for index, shift in enumerate(shifts):
        step, layer_index = divmod(index, per_section)
        params = (
            vectors[step, layer_index],
            matrices[step, 3 * layer_index : 3 * layer_index + 3],
            vectors[step, per_section + layer_index],
            matrices[step, 3 * per_section + layer_index],
            shift,
        )
        if index < REDUNDANT:
            x = widened_layer(x, *params)
        else:
            x = exchanged_layer(x, *params)
        if layer_index == per_section - 1:
            edge = (x.shape[0] - chunk) // 2
            gathered = lax.all_gather(x[edge : edge + chunk], "section")
            result = gathered if result is None else jnp.where(my_section == step, gathered, result)
    result = result.reshape(n_section, runs, group, channels).transpose(1, 0, 2, 3)
    return result.reshape(1, block, channels)


def solution(mesh):
    in_specs = (
        P("pos", None),
        P("section", None, None),
        P("section", None, None, None, None),
        P("section", None, None),
        P("section", None, None, None),
    )
    out_specs = P("section", "pos", None)
    return jax.shard_map(body, mesh=mesh, in_specs=in_specs, out_specs=out_specs, check_vma=False)
```

profile of v0, /device:TPU:1, one launch (start us, length us, event | category | flops | bytes accessed | tf_op | source)
XLA Modules:
  0.0 166.9 jit_solution(2590244490608321159)
XLA Ops:
  6.5 1.7 %pad_maximum_fusion.1 = bf16[1,8,128,128]{3,2,1,0:T(8,128)(2,1)} fusion(bf16[1,2,128,128]{3,2,1,0:T(8,128)(2,1)} %param.9, bf16[1,6,128,128]{3,2,1,0:T(8,128)(2,1)} %bitcast.185), kind=kLoop, calls=%fused_computation.544 | loop fusion | flops 131072 | bytes 524288 | tf_op jit(solution)/shard_map/concatenate | solution.py:64
  9.4 2.5 %collective-permute-start = (bf16[248,128]{1,0:T(8,128)(2,1)S(1)}, bf16[248,128]{1,0:T(8,128)(2,1)S(1)}, u32[]{:S(2)}, u32[]{:S(2)}) collective-permute-start(bf16[248,128]{1,0:T(8,128)(2,1)S(1)} %get-tuple-element.15), channel_id=1, source_target_pairs={{0,4},{4,8},{8,12},{12,16},{16,20},{20,24},{24,28},{28,32},{32,36}... | collective-permute-start | bytes 190472 | tf_op jit(solution)/shard_map/ppermute | solution.py:11
  11.9 8.9 %collective-permute-start.1 = (bf16[248,128]{1,0:T(8,128)(2,1)S(1)}, bf16[248,128]{1,0:T(8,128)(2,1)S(1)}, u32[]{:S(2)}, u32[]{:S(2)}) collective-permute-start(bf16[248,128]{1,0:T(8,128)(2,1)S(1)} %get-tuple-element.16), channel_id=1, source_target_pairs={{0,252},{4,0},{8,4},{12,8},{16,12},{20,16},{24,20},{28,24},{32,28}... | collective-permute-start | bytes 190472 | tf_op jit(solution)/shard_map/ppermute | solution.py:11
  20.8 6.0 %all_gather.30 = f32[4,4,128]{2,1,0:T(4,128)S(1)} all-gather(f32[1,4,128]{2,1,0:T(4,128)S(1)} %pad_maximum_fusion.2), channel_id=1, replica_groups=mesh['pos'=64,'section'=4] {'section'}, dimensions={0}, use_global_device_ids=true | all-gather | bytes 10240 | tf_op jit(solution)/shard_map/all_gather | solution.py:73
  27.1 2.2 %fusion.22 = bf16[1520,128]{1,0:T(8,128)(2,1)S(1)} fusion(bf16[1520,128]{1,0:T(8,128)(2,1)S(1)} %get-tuple-element.6, f32[128]{0:T(128)S(1)} %get-tuple-element.32, f32[1520]{0:T(1024)S(1)} %add_rsqrt_fusion.4), kind=kLoop, calls=%fused_computation.74 | loop fusion | flops 13230080 | bytes 784832 | tf_op jit(solution)/shard_map/convert_element_type | solution.py:17
  29.3 7.3 %all-gather.10.cloned.1.call-done = bf16[4,8,128,128]{3,2,1,0:T(8,128)(2,1)} async-done(((bf16[1,8,128,128]{3,2,1,0:T(8,128)(2,1)}), bf16[4,8,128,128]{3,2,1,0:T(8,128)(2,1)}) %all-gather.10.cloned.1.call-update) | async-done | bytes 1048592 | tf_op jit(solution)/shard_map/all_gather | solution.py:72
  38.1 2.2 %fusion.41 = (f32[1504]{0:T(1024)S(1)}, bf16[1504,128]{1,0:T(8,128)(2,1)S(1)}) fusion(bf16[4,8,128,128]{3,2,1,0:T(8,128)(2,1)S(1)} %copy-done.2, f32[1504,128]{1,0:T(8,128)S(1)} %convolution_add_fusion.10, bf16[1520,128]{1,0:T(8,128)(2,1)S(1)} %fusion.22, f32[128]{0:T(128)S(1)} %get-tuple-element.31, bf16[1520,128]{1,0:T(8,128)(2,1)S(1)} %get-tuple-element.6), kind=kOutput, calls=%fused_computation.93 | convolution fusion | flops 112618016 | bytes 1997184 | tf_op jit(solution)/shard_map/dot_general | solution.py:25
  40.3 2.2 %fusion.46 = bf16[1504,128]{1,0:T(8,128)(2,1)S(1)} fusion(bf16[1504,128]{1,0:T(8,128)(2,1)S(1)} %get-tuple-element.34, f32[128]{0:T(128)S(1)} %get-tuple-element.30, f32[1504]{0:T(1024)S(1)} %add_rsqrt_fusion.3), kind=kLoop, calls=%fused_computation.98 | loop fusion | flops 13090816 | bytes 776576 | tf_op jit(solution)/shard_map/convert_element_type | solution.py:17
  43.0 2.2 %fusion.76 = (f32[1472]{0:T(1024)S(1)}, bf16[1472,128]{1,0:T(8,128)(2,1)S(1)}) fusion(bf16[4,8,128,128]{3,2,1,0:T(8,128)(2,1)S(1)} %copy-done.2, f32[1472,128]{1,0:T(8,128)S(1)} %convolution_add_fusion.8, bf16[1504,128]{1,0:T(8,128)(2,1)S(1)} %fusion.46, f32[128]{0:T(128)S(1)} %get-tuple-element.29, bf16[1504,128]{1,0:T(8,128)(2,1)S(1)} %get-tuple-element.34), kind=kOutput, calls=%fused_computation.137 | convolution fusion | flops 110221888 | bytes 1956096 | tf_op jit(solution)/shard_map/dot_general | solution.py:25
  45.9 2.3 %fusion.81 = bf16[1472,128]{1,0:T(8,128)(2,1)S(1)} fusion(bf16[1472,128]{1,0:T(8,128)(2,1)S(1)} %get-tuple-element.36, f32[128]{0:T(128)S(1)} %get-tuple-element.28, f32[1472]{0:T(1024)S(1)} %add_rsqrt_fusion.2), kind=kLoop, calls=%fused_computation.142 | loop fusion | flops 12812288 | bytes 760064 | tf_op jit(solution)/shard_map/convert_element_type | solution.py:17
  48.6 2.0 %fusion.110 = (f32[1408]{0:T(1024)S(1)}, bf16[1408,128]{1,0:T(8,128)(2,1)S(1)}) fusion(bf16[4,8,128,128]{3,2,1,0:T(8,128)(2,1)S(1)} %copy-done.2, f32[1408,128]{1,0:T(8,128)S(1)} %convolution_add_fusion.5, bf16[1472,128]{1,0:T(8,128)(2,1)S(1)} %fusion.81, f32[128]{0:T(128)S(1)} %get-tuple-element.27, bf16[1472,128]{1,0:T(8,128)(2,1)S(1)} %get-tuple-element.36), kind=kOutput, calls=%fused_computation.179 | convolution fusion | flops 105429632 | bytes 1873920 | tf_op jit(solution)/shard_map/dot_general | solution.py:25
  50.7 1.7 %fusion.115 = bf16[1408,128]{1,0:T(8,128)(2,1)S(1)} fusion(bf16[1408,128]{1,0:T(8,128)(2,1)S(1)} %get-tuple-element.38, f32[128]{0:T(128)S(1)} %get-tuple-element.26, f32[1408]{0:T(1024)S(1)} %add_rsqrt_fusion.1), kind=kLoop, calls=%fused_computation.184 | loop fusion | flops 12255232 | bytes 727040 | tf_op jit(solution)/shard_map/convert_element_type | solution.py:17
  52.9 1.9 %fusion.144 = (f32[1280]{0:T(1024)S(1)}, bf16[1280,128]{1,0:T(8,128)(2,1)S(1)}) fusion(bf16[4,8,128,128]{3,2,1,0:T(8,128)(2,1)S(1)} %copy-done.2, f32[1280,128]{1,0:T(8,128)S(1)} %convolution_add_fusion.2, bf16[1408,128]{1,0:T(8,128)(2,1)S(1)} %fusion.115, f32[128]{0:T(128)S(1)} %get-tuple-element.25, bf16[1408,128]{1,0:T(8,128)(2,1)S(1)} %get-tuple-element.38), kind=kOutput, calls=%fused_computation.221 | convolution fusion | flops 95845120 | bytes 1709568 | tf_op jit(solution)/shard_map/dot_general | solution.py:25
  61.7 6.4 %collective-permute-start.3 = (bf16[256,128]{1,0:T(8,128)(2,1)S(1)}, bf16[256,128]{1,0:T(8,128)(2,1)S(1)}, u32[]{:S(2)}, u32[]{:S(2)}) collective-permute-start(bf16[256,128]{1,0:T(8,128)(2,1)S(1)} %get-tuple-element.13), channel_id=1, source_target_pairs={{0,252},{4,0},{8,4},{12,8},{16,12},{20,16},{24,20},{28,24},{32,28}... | collective-permute-start | bytes 196616 | tf_op jit(solution)/shard_map/ppermute | solution.py:11
  68.3 1.9 %collective-permute-done.2 = bf16[256,128]{1,0:T(8,128)(2,1)S(1)} collective-permute-done((bf16[256,128]{1,0:T(8,128)(2,1)S(1)}, bf16[256,128]{1,0:T(8,128)(2,1)S(1)}, u32[]{:S(2)}, u32[]{:S(2)}) %collective-permute-start.2) | collective-permute-done | bytes 65568 | tf_op jit(solution)/shard_map/ppermute | solution.py:11
  70.4 1.6 fusion.187
  73.4 7.2 %collective-permute-start.5 = (bf16[512,128]{1,0:T(8,128)(2,1)S(1)}, bf16[512,128]{1,0:T(8,128)(2,1)S(1)}, u32[]{:S(2)}, u32[]{:S(2)}) collective-permute-start(bf16[512,128]{1,0:T(8,128)(2,1)S(1)} %get-tuple-element.10), channel_id=1, source_target_pairs={{0,252},{4,0},{8,4},{12,8},{16,12},{20,16},{24,20},{28,24},{32,28}... | collective-permute-start | bytes 393224 | tf_op jit(solution)/shard_map/ppermute | solution.py:11
  80.9 2.7 %collective-permute-done.4 = bf16[512,128]{1,0:T(8,128)(2,1)S(1)} collective-permute-done((bf16[512,128]{1,0:T(8,128)(2,1)S(1)}, bf16[512,128]{1,0:T(8,128)(2,1)S(1)}, u32[]{:S(2)}, u32[]{:S(2)}) %collective-permute-start.4) | collective-permute-done | bytes 131104 | tf_op jit(solution)/shard_map/ppermute | solution.py:11
  86.8 7.2 %collective-permute-start.7 = (bf16[1024,128]{1,0:T(8,128)(2,1)S(1)}, bf16[1024,128]{1,0:T(8,128)(2,1)S(1)}, u32[]{:S(2)}, u32[]{:S(2)}) collective-permute-start(bf16[1024,128]{1,0:T(8,128)(2,1)S(1)} %fusion.205), channel_id=1, source_target_pairs={{0,252},{4,0},{8,4},{12,8},{16,12},{20,16},{24,20},{28,24},{32,28}... | collective-permute-start | bytes 786440 | tf_op jit(solution)/shard_map/ppermute | solution.py:11
  94.2 4.8 %collective-permute-done.6 = bf16[1024,128]{1,0:T(8,128)(2,1)S(1)} collective-permute-done((bf16[1024,128]{1,0:T(8,128)(2,1)S(1)}, bf16[1024,128]{1,0:T(8,128)(2,1)S(1)}, u32[]{:S(2)}, u32[]{:S(2)}) %collective-permute-start.6) | collective-permute-done | bytes 262176 | tf_op jit(solution)/shard_map/ppermute | solution.py:11
  99.2 2.2 %fusion.16 = bf16[1024,128]{1,0:T(8,128)(2,1)} fusion(f32[1024,128]{1,0:T(8,128)S(1)} %get-tuple-element.46, f32[1024,128]{1,0:T(8,128)S(1)} %convolution_add_fusion.13, bf16[1024,128]{1,0:T(8,128)(2,1)S(1)} %collective-permute-done.7, f32[128]{0:T(128)S(1)} %get-tuple-element.17, bf16[4,8,128,128]{3,2,1,0:T(8,128)(2,1)S(1)} %copy-done.2), kind=kOutput, calls=%fused_computation.39 | convolution fusion | flops 76152832 | bytes 1638912 | tf_op jit(solution)/shard_map/dot_general | solution.py:25
  101.4 4.8 %all-gather.18.cloned.1.call-done = bf16[4096,128]{1,0:T(8,128)(2,1)} async-done(((bf16[1024,128]{1,0:T(8,128)(2,1)}), bf16[4096,128]{1,0:T(8,128)(2,1)}) %all-gather.18.cloned.1.call-update) | async-done | bytes 1048592 | tf_op jit(solution)/shard_map/all_gather | solution.py:99
  106.2 25.7 %all-gather.14.cloned.1.call-done = bf16[4096,128]{1,0:T(8,128)(2,1)} async-done(((bf16[1024,128]{1,0:T(8,128)(2,1)}), bf16[4096,128]{1,0:T(8,128)(2,1)}) %all-gather.14.cloned.1.call-update) | async-done | bytes 1048592 | tf_op jit(solution)/shard_map/all_gather | solution.py:99
  132.0 25.8 %all-gather.12.cloned.1.call-done = bf16[4096,128]{1,0:T(8,128)(2,1)} async-done(((bf16[1024,128]{1,0:T(8,128)(2,1)}), bf16[4096,128]{1,0:T(8,128)(2,1)}) %all-gather.12.cloned.1.call-update) | async-done | bytes 1048592 | tf_op jit(solution)/shard_map/all_gather | solution.py:99
  (71 shorter events, 20.1 us)
Async XLA Ops:
  6.5 30.1 %all-gather.10.cloned.1.call-start = ((), (), s32[]{:S(2)}) async-start(), calls=%async_computation | async-start | bytes 1310720 | tf_op jit(solution)/shard_map/all_gather | solution.py:72
  8.3 93.2 %all-gather.16.cloned.1.call-start = ((), (), s32[]{:S(2)}) async-start(), calls=%async_computation.3 | async-start | bytes 1310720 | tf_op jit(solution)/shard_map/all_gather | solution.py:99
  9.4 11.4 %copy-start.4 = (f32[1,2,128]{2,1,0:T(2,128)S(1)}, f32[1,2,128]{2,1,0:T(2,128)}, u32[]{:S(2)}) copy-start(f32[1,2,128]{2,1,0:T(2,128)} %param.6) | copy-start | bytes 3076
  9.4 11.4 %copy-start.3 = (f32[1,2,128]{2,1,0:T(2,128)S(1)}, f32[1,2,128]{2,1,0:T(2,128)}, u32[]{:S(2)}) copy-start(f32[1,2,128]{2,1,0:T(2,128)} %param.8) | copy-start | bytes 3076
  9.4 17.4 %collective-permute-start = (bf16[248,128]{1,0:T(8,128)(2,1)S(1)}, bf16[248,128]{1,0:T(8,128)(2,1)S(1)}, u32[]{:S(2)}, u32[]{:S(2)}) collective-permute-start(bf16[248,128]{1,0:T(8,128)(2,1)S(1)} %get-tuple-element.15), channel_id=1, source_target_pairs={{0,4},{4,8},{8,12},{12,16},{16,20},{20,24},{24,28},{28,32},{32,36}... | collective-permute-start | bytes 190472 | tf_op jit(solution)/shard_map/ppermute | solution.py:11
  11.9 14.9 %collective-permute-start.1 = (bf16[248,128]{1,0:T(8,128)(2,1)S(1)}, bf16[248,128]{1,0:T(8,128)(2,1)S(1)}, u32[]{:S(2)}, u32[]{:S(2)}) collective-permute-start(bf16[248,128]{1,0:T(8,128)(2,1)S(1)} %get-tuple-element.16), channel_id=1, source_target_pairs={{0,252},{4,0},{8,4},{12,8},{16,12},{20,16},{24,20},{28,24},{32,28}... | collective-permute-start | bytes 190472 | tf_op jit(solution)/shard_map/ppermute | solution.py:11
  36.6 1.2 copy-start.2
  55.5 50.7 %all-gather.18.cloned.1.call-start = ((), (), s32[]{:S(2)}) async-start(), calls=%async_computation.4 | async-start | bytes 1310720 | tf_op jit(solution)/shard_map/all_gather | solution.py:99
  60.3 9.9 %collective-permute-start.2 = (bf16[256,128]{1,0:T(8,128)(2,1)S(1)}, bf16[256,128]{1,0:T(8,128)(2,1)S(1)}, u32[]{:S(2)}, u32[]{:S(2)}) collective-permute-start(bf16[256,128]{1,0:T(8,128)(2,1)S(1)} %get-tuple-element.14), channel_id=1, source_target_pairs={{0,4},{4,8},{8,12},{12,16},{16,20},{20,24},{24,28},{28,32},{32,36}... | collective-permute-start | bytes 196616 | tf_op jit(solution)/shard_map/ppermute | solution.py:11
  61.7 8.8 %collective-permute-start.3 = (bf16[256,128]{1,0:T(8,128)(2,1)S(1)}, bf16[256,128]{1,0:T(8,128)(2,1)S(1)}, u32[]{:S(2)}, u32[]{:S(2)}) collective-permute-start(bf16[256,128]{1,0:T(8,128)(2,1)S(1)} %get-tuple-element.13), channel_id=1, source_target_pairs={{0,252},{4,0},{8,4},{12,8},{16,12},{20,16},{24,20},{28,24},{32,28}... | collective-permute-start | bytes 196616 | tf_op jit(solution)/shard_map/ppermute | solution.py:11
  68.1 63.9 %all-gather.14.cloned.1.call-start = ((), (), s32[]{:S(2)}) async-start(), calls=%async_computation.2 | async-start | bytes 1310720 | tf_op jit(solution)/shard_map/all_gather | solution.py:99
  72.0 1.3 copy-start
  73.3 10.3 %collective-permute-start.4 = (bf16[512,128]{1,0:T(8,128)(2,1)S(1)}, bf16[512,128]{1,0:T(8,128)(2,1)S(1)}, u32[]{:S(2)}, u32[]{:S(2)}) collective-permute-start(bf16[512,128]{1,0:T(8,128)(2,1)S(1)} %get-tuple-element.9), channel_id=1, source_target_pairs={{0,4},{4,8},{8,12},{12,16},{16,20},{20,24},{24,28},{28,32},{32,36}... | collective-permute-start | bytes 393224 | tf_op jit(solution)/shard_map/ppermute | solution.py:11
  73.4 10.4 %collective-permute-start.5 = (bf16[512,128]{1,0:T(8,128)(2,1)S(1)}, bf16[512,128]{1,0:T(8,128)(2,1)S(1)}, u32[]{:S(2)}, u32[]{:S(2)}) collective-permute-start(bf16[512,128]{1,0:T(8,128)(2,1)S(1)} %get-tuple-element.10), channel_id=1, source_target_pairs={{0,252},{4,0},{8,4},{12,8},{16,12},{20,16},{24,20},{28,24},{32,28}... | collective-permute-start | bytes 393224 | tf_op jit(solution)/shard_map/ppermute | solution.py:11
  80.7 77.1 %all-gather.12.cloned.1.call-start = ((), (), s32[]{:S(2)}) async-start(), calls=%async_computation.1 | async-start | bytes 1310720 | tf_op jit(solution)/shard_map/all_gather | solution.py:99
  80.9 2.9 %copy-start.1 = (bf16[1024,128]{1,0:T(8,128)(2,1)S(1)}, bf16[1024,128]{1,0:T(8,128)(2,1)}, u32[]{:S(2)}) copy-start(bf16[1024,128]{1,0:T(8,128)(2,1)} %copy-done) | copy-start | bytes 786436
  86.7 12.3 %collective-permute-start.6 = (bf16[1024,128]{1,0:T(8,128)(2,1)S(1)}, bf16[1024,128]{1,0:T(8,128)(2,1)S(1)}, u32[]{:S(2)}, u32[]{:S(2)}) collective-permute-start(bf16[1024,128]{1,0:T(8,128)(2,1)S(1)} %fusion.205), channel_id=1, source_target_pairs={{0,4},{4,8},{8,12},{12,16},{16,20},{20,24},{24,28},{28,32},{32,36}... | collective-permute-start | bytes 786440 | tf_op jit(solution)/shard_map/ppermute | solution.py:11
  86.8 12.4 %collective-permute-start.7 = (bf16[1024,128]{1,0:T(8,128)(2,1)S(1)}, bf16[1024,128]{1,0:T(8,128)(2,1)S(1)}, u32[]{:S(2)}, u32[]{:S(2)}) collective-permute-start(bf16[1024,128]{1,0:T(8,128)(2,1)S(1)} %fusion.205), channel_id=1, source_target_pairs={{0,252},{4,0},{8,4},{12,8},{16,12},{20,16},{24,20},{28,24},{32,28}... | collective-permute-start | bytes 786440 | tf_op jit(solution)/shard_map/ppermute | solution.py:11
Sparse Core Ops, SparseCore 0:
  9.1 27.4 all-gather.9
  55.6 26.8 all-gather.15
  84.4 21.8 all-gather.17
  107.9 24.0 all-gather.13
  133.6 24.0 all-gather.11
where the time goes:
time: 167 us
  waiting for transfers between devices  73.1 us (44%)
  starting transfers between devices  33.8 us (20%)
  matrix products  19.5 us (12%)
  other arithmetic  17.1 us (10%)
  between operations  13.5 us (8%)
  blocking collectives  5.98 us (4%)
  local copies, waits for them, and re-layouts  3.88 us (2%)
    all_gather x4, waiting for transfers between devices, body(): gathered = lax.all_gather(x[edge:edge + chunk], 'section')  56.4 us
    ppermute x8, starting transfers between devices, shifted(): lax.ppermute(block, 'pos', [(i, (i + shift) % count) for i in range(count)])  33.6 us
    dot_general x8, matrix products, mix(): jnp.dot(g, mixing, preferred_element_type=jnp.float32)  15.2 us
    convert_element_type x8, other arithmetic, prepare(): jax.nn.gelu(r * lax.rsqrt(meansq + 1e-06) * gain, approximate=False)  13.6 us
    ppermute x8, waiting for transfers between devices, shifted(): lax.ppermute(block, 'pos', [(i, (i + shift) % count) for i in range(count)])  9.34 us
    all_gather x1, waiting for transfers between devices, body(): matrices = lax.all_gather(matrices, 'section', tiled=True)  7.3 us
    all_gather x1, blocking collectives, body(): vectors = lax.all_gather(vectors, 'section', tiled=True)  5.98 us
  transfers between devices with their start and end apart: 13, of which 7 were waited for; matrix products, arithmetic and copies ran while one was open for 10% of the time, Pallas kernels for 0%

commit v1 on v0

--- a/solution.py
+++ b/solution.py
@@ -69,7 +69,10 @@
         axis=1,
     )
     vectors = jnp.concatenate([norm_gain, conv_bias], axis=1)
-    matrices = lax.all_gather(matrices, "section", tiled=True)
+    devices = lax.axis_size("section")
+    blocks = jnp.stack([matrices for _ in range(devices)])
+    blocks = lax.all_to_all(blocks, "section", split_axis=0, concat_axis=0)
+    matrices = jnp.concatenate(blocks, axis=0)
     vectors = lax.all_gather(vectors, "section", tiled=True)
     runs_of = sequence_features.reshape(runs, n_section, group, channels)
     x = lax.dynamic_index_in_dim(runs_of, my_section, axis=1, keepdims=False).reshape(

time: 167 us -> 169 us (1.012)
  waiting for transfers between devices: 73.1 us -> 62.8 us
  blocking collectives: 5.98 us -> 15.2 us
  starting transfers between devices: 33.8 us -> 38.4 us
  other arithmetic: 17.1 us -> 15.4 us
    all_gather x1, blocking collectives: 5.98 us -> 15.2 us  [body(): vectors = lax.all_gather(vectors, 'section', tiled=True)]
    all_gather x1 -> x0, waiting for transfers between devices: 7.3 us -> none  [body(): matrices = lax.all_gather(matrices, 'section', tiled=True)]
    all_to_all x0 -> x1, starting transfers between devices: none -> 4.57 us  [body(): blocks = lax.all_to_all(blocks, 'section', split_axis=0, concat_axis=0)]
    ppermute x8, waiting for transfers between devices: 9.34 us -> 6.67 us  [shifted(): lax.ppermute(block, 'pos', [(i, (i + shift) % count) for i in range(count)])]
where the time goes in v1:
time: 169 us
  waiting for transfers between devices  62.8 us (37%)
  starting transfers between devices  38.4 us (23%)
  matrix products  18.7 us (11%)
  other arithmetic  15.4 us (9%)
  blocking collectives  15.2 us (9%)
  between operations  13.5 us (8%)
  local copies, waits for them, and re-layouts  4.96 us (3%)
    all_gather x4, waiting for transfers between devices, body(): gathered = lax.all_gather(x[edge:edge + chunk], 'section')  56.1 us
    ppermute x8, starting transfers between devices, shifted(): lax.ppermute(block, 'pos', [(i, (i + shift) % count) for i in range(count)])  33.7 us
    all_gather x1, blocking collectives, body(): vectors = lax.all_gather(vectors, 'section', tiled=True)  15.2 us
    dot_general x8, matrix products, mix(): jnp.dot(g, mixing, preferred_element_type=jnp.float32)  15.2 us
    convert_element_type x8, other arithmetic, prepare(): jax.nn.gelu(r * lax.rsqrt(meansq + 1e-06) * gain, approximate=False)  13.6 us
    ppermute x8, waiting for transfers between devices, shifted(): lax.ppermute(block, 'pos', [(i, (i + shift) % count) for i in range(count)])  6.67 us
    all_to_all x1, starting transfers between devices, body(): blocks = lax.all_to_all(blocks, 'section', split_axis=0, concat_axis=0)  4.57 us
  transfers between devices with their start and end apart: 13, of which 7 were waited for; matrix products, arithmetic and copies ran while one was open for 10% of the time, Pallas kernels for 0%

profile of v1, /device:TPU:1, one launch (start us, length us, event | category | flops | bytes accessed | tf_op | source)
XLA Modules:
  0.0 169.0 jit_solution(7989595870405644881)
XLA Ops:
  7.6 2.5 %collective-permute-start = (bf16[248,128]{1,0:T(8,128)(2,1)S(1)}, bf16[248,128]{1,0:T(8,128)(2,1)S(1)}, u32[]{:S(2)}, u32[]{:S(2)}) collective-permute-start(bf16[248,128]{1,0:T(8,128)(2,1)S(1)} %get-tuple-element.15), channel_id=1, source_target_pairs={{0,4},{4,8},{8,12},{12,16},{16,20},{20,24},{24,28},{28,32},{32,36}... | collective-permute-start | bytes 190472 | tf_op jit(solution)/shard_map/ppermute | solution.py:11
  10.2 8.9 %collective-permute-start.1 = (bf16[248,128]{1,0:T(8,128)(2,1)S(1)}, bf16[248,128]{1,0:T(8,128)(2,1)S(1)}, u32[]{:S(2)}, u32[]{:S(2)}) collective-permute-start(bf16[248,128]{1,0:T(8,128)(2,1)S(1)} %get-tuple-element.16), channel_id=1, source_target_pairs={{0,252},{4,0},{8,4},{12,8},{16,12},{20,16},{24,20},{28,24},{32,28}... | collective-permute-start | bytes 190472 | tf_op jit(solution)/shard_map/ppermute | solution.py:11
  20.3 4.6 %all-to-all-start = ((bf16[4,1,8,128,128]{4,3,2,1,0:T(8,128)(2,1)}), bf16[4,1,8,128,128]{4,3,2,1,0:T(8,128)(2,1)S(1)}, u32[]{:S(2)}, u32[]{:S(2)}) async-start(bf16[4,1,8,128,128]{4,3,2,1,0:T(8,128)(2,1)} %stack.2), calls=%async_computation | async-start | bytes 2097152 | tf_op jit(solution)/shard_map/all_to_all | solution.py:74
  24.9 15.2 %all_gather.27 = f32[4,4,128]{2,1,0:T(4,128)S(1)} all-gather(f32[1,4,128]{2,1,0:T(4,128)S(1)} %pad_maximum_fusion.1), channel_id=1, replica_groups=mesh['pos'=64,'section'=4] {'section'}, dimensions={0}, use_global_device_ids=true | all-gather | bytes 10240 | tf_op jit(solution)/shard_map/all_gather | solution.py:76
  40.4 2.2 %fusion.22 = bf16[1520,128]{1,0:T(8,128)(2,1)S(1)} fusion(bf16[1520,128]{1,0:T(8,128)(2,1)S(1)} %get-tuple-element.6, f32[128]{0:T(128)S(1)} %get-tuple-element.32, f32[1520]{0:T(1024)S(1)} %add_rsqrt_fusion.4), kind=kLoop, calls=%fused_computation.74 | loop fusion | flops 13230080 | bytes 784832 | tf_op jit(solution)/shard_map/convert_element_type | solution.py:17
  43.1 2.2 %fusion.41 = (f32[1504]{0:T(1024)S(1)}, bf16[1504,128]{1,0:T(8,128)(2,1)S(1)}) fusion(bf16[4,8,128,128]{3,2,1,0:T(8,128)(2,1)S(1)} %bitcast.190, f32[1504,128]{1,0:T(8,128)S(1)} %convolution_add_fusion.10, bf16[1520,128]{1,0:T(8,128)(2,1)S(1)} %fusion.22, f32[128]{0:T(128)S(1)} %get-tuple-element.31, bf16[1520,128]{1,0:T(8,128)(2,1)S(1)} %get-tuple-element.6), kind=kOutput, calls=%fused_computation.93 | convolution fusion | flops 112618016 | bytes 1997184 | tf_op jit(solution)/shard_map/dot_general | solution.py:25
  45.3 2.2 %fusion.46 = bf16[1504,128]{1,0:T(8,128)(2,1)S(1)} fusion(bf16[1504,128]{1,0:T(8,128)(2,1)S(1)} %get-tuple-element.34, f32[128]{0:T(128)S(1)} %get-tuple-element.30, f32[1504]{0:T(1024)S(1)} %add_rsqrt_fusion.3), kind=kLoop, calls=%fused_computation.98 | loop fusion | flops 13090816 | bytes 776576 | tf_op jit(solution)/shard_map/convert_element_type | solution.py:17
  48.0 2.2 %fusion.76 = (f32[1472]{0:T(1024)S(1)}, bf16[1472,128]{1,0:T(8,128)(2,1)S(1)}) fusion(bf16[4,8,128,128]{3,2,1,0:T(8,128)(2,1)S(1)} %bitcast.193, f32[1472,128]{1,0:T(8,128)S(1)} %convolution_add_fusion.8, bf16[1504,128]{1,0:T(8,128)(2,1)S(1)} %fusion.46, f32[128]{0:T(128)S(1)} %get-tuple-element.29, bf16[1504,128]{1,0:T(8,128)(2,1)S(1)} %get-tuple-element.34), kind=kOutput, calls=%fused_computation.137 | convolution fusion | flops 110221888 | bytes 1956096 | tf_op jit(solution)/shard_map/dot_general | solution.py:25
  50.2 2.3 %fusion.81 = bf16[1472,128]{1,0:T(8,128)(2,1)S(1)} fusion(bf16[1472,128]{1,0:T(8,128)(2,1)S(1)} %get-tuple-element.36, f32[128]{0:T(128)S(1)} %get-tuple-element.28, f32[1472]{0:T(1024)S(1)} %add_rsqrt_fusion.2), kind=kLoop, calls=%fused_computation.142 | loop fusion | flops 12812288 | bytes 760064 | tf_op jit(solution)/shard_map/convert_element_type | solution.py:17
  53.0 2.0 %fusion.110 = (f32[1408]{0:T(1024)S(1)}, bf16[1408,128]{1,0:T(8,128)(2,1)S(1)}) fusion(bf16[4,8,128,128]{3,2,1,0:T(8,128)(2,1)S(1)} %bitcast.196, f32[1408,128]{1,0:T(8,128)S(1)} %convolution_add_fusion.5, bf16[1472,128]{1,0:T(8,128)(2,1)S(1)} %fusion.81, f32[128]{0:T(128)S(1)} %get-tuple-element.27, bf16[1472,128]{1,0:T(8,128)(2,1)S(1)} %get-tuple-element.36), kind=kOutput, calls=%fused_computation.179 | convolution fusion | flops 105429632 | bytes 1873920 | tf_op jit(solution)/shard_map/dot_general | solution.py:25
  55.1 1.7 fusion.115
  57.2 1.9 %fusion.144 = (f32[1280]{0:T(1024)S(1)}, bf16[1280,128]{1,0:T(8,128)(2,1)S(1)}) fusion(bf16[4,8,128,128]{3,2,1,0:T(8,128)(2,1)S(1)} %bitcast.199, f32[1280,128]{1,0:T(8,128)S(1)} %convolution_add_fusion.2, bf16[1408,128]{1,0:T(8,128)(2,1)S(1)} %fusion.115, f32[128]{0:T(128)S(1)} %get-tuple-element.25, bf16[1408,128]{1,0:T(8,128)(2,1)S(1)} %get-tuple-element.38), kind=kOutput, calls=%fused_computation.221 | convolution fusion | flops 95845120 | bytes 1709568 | tf_op jit(solution)/shard_map/dot_general | solution.py:25
  61.9 1.6 multiply_reduce_fusion.1
  65.8 7.2 %collective-permute-start.3 = (bf16[256,128]{1,0:T(8,128)(2,1)S(1)}, bf16[256,128]{1,0:T(8,128)(2,1)S(1)}, u32[]{:S(2)}, u32[]{:S(2)}) collective-permute-start(bf16[256,128]{1,0:T(8,128)(2,1)S(1)} %get-tuple-element.13), channel_id=1, source_target_pairs={{0,252},{4,0},{8,4},{12,8},{16,12},{20,16},{24,20},{28,24},{32,28}... | collective-permute-start | bytes 196616 | tf_op jit(solution)/shard_map/ppermute | solution.py:11
  74.3 1.6 fusion.187
  77.2 7.7 %collective-permute-start.5 = (bf16[512,128]{1,0:T(8,128)(2,1)S(1)}, bf16[512,128]{1,0:T(8,128)(2,1)S(1)}, u32[]{:S(2)}, u32[]{:S(2)}) collective-permute-start(bf16[512,128]{1,0:T(8,128)(2,1)S(1)} %get-tuple-element.10), channel_id=1, source_target_pairs={{0,252},{4,0},{8,4},{12,8},{16,12},{20,16},{24,20},{28,24},{32,28}... | collective-permute-start | bytes 393224 | tf_op jit(solution)/shard_map/ppermute | solution.py:11
  85.2 2.0 %collective-permute-done.4 = bf16[512,128]{1,0:T(8,128)(2,1)S(1)} collective-permute-done((bf16[512,128]{1,0:T(8,128)(2,1)S(1)}, bf16[512,128]{1,0:T(8,128)(2,1)S(1)}, u32[]{:S(2)}, u32[]{:S(2)}) %collective-permute-start.4) | collective-permute-done | bytes 131104 | tf_op jit(solution)/shard_map/ppermute | solution.py:11
  87.4 1.6 multiply_reduce_fusion
  90.3 7.2 %collective-permute-start.7 = (bf16[1024,128]{1,0:T(8,128)(2,1)S(1)}, bf16[1024,128]{1,0:T(8,128)(2,1)S(1)}, u32[]{:S(2)}, u32[]{:S(2)}) collective-permute-start(bf16[1024,128]{1,0:T(8,128)(2,1)S(1)} %fusion.205), channel_id=1, source_target_pairs={{0,252},{4,0},{8,4},{12,8},{16,12},{20,16},{24,20},{28,24},{32,28}... | collective-permute-start | bytes 786440 | tf_op jit(solution)/shard_map/ppermute | solution.py:11
  97.7 3.6 %collective-permute-done.6 = bf16[1024,128]{1,0:T(8,128)(2,1)S(1)} collective-permute-done((bf16[1024,128]{1,0:T(8,128)(2,1)S(1)}, bf16[1024,128]{1,0:T(8,128)(2,1)S(1)}, u32[]{:S(2)}, u32[]{:S(2)}) %collective-permute-start.6) | collective-permute-done | bytes 262176 | tf_op jit(solution)/shard_map/ppermute | solution.py:11
  101.6 2.2 %fusion.16 = bf16[1024,128]{1,0:T(8,128)(2,1)} fusion(f32[1024,128]{1,0:T(8,128)S(1)} %get-tuple-element.46, f32[1024,128]{1,0:T(8,128)S(1)} %convolution_add_fusion.13, bf16[1024,128]{1,0:T(8,128)(2,1)S(1)} %collective-permute-done.7, f32[128]{0:T(128)S(1)} %get-tuple-element.17, bf16[4,8,128,128]{3,2,1,0:T(8,128)(2,1)S(1)} %bitcast.211), kind=kOutput, calls=%fused_computation.39 | convolution fusion | flops 76152832 | bytes 1638912 | tf_op jit(solution)/shard_map/dot_general | solution.py:25
  103.9 3.1 %all-gather.15.cloned.1.call-done = bf16[4096,128]{1,0:T(8,128)(2,1)} async-done(((bf16[1024,128]{1,0:T(8,128)(2,1)}), bf16[4096,128]{1,0:T(8,128)(2,1)}) %all-gather.15.cloned.1.call-update) | async-done | bytes 1048592 | tf_op jit(solution)/shard_map/all_gather | solution.py:102
  107.0 27.2 %all-gather.11.cloned.1.call-done = bf16[4096,128]{1,0:T(8,128)(2,1)} async-done(((bf16[1024,128]{1,0:T(8,128)(2,1)}), bf16[4096,128]{1,0:T(8,128)(2,1)}) %all-gather.11.cloned.1.call-update) | async-done | bytes 1048592 | tf_op jit(solution)/shard_map/all_gather | solution.py:102
  134.1 25.8 %all-gather.9.cloned.1.call-done = bf16[4096,128]{1,0:T(8,128)(2,1)} async-done(((bf16[1024,128]{1,0:T(8,128)(2,1)}), bf16[4096,128]{1,0:T(8,128)(2,1)}) %all-gather.9.cloned.1.call-update) | async-done | bytes 1048592 | tf_op jit(solution)/shard_map/all_gather | solution.py:102
  (73 shorter events, 17.0 us)
Async XLA Ops:
  6.5 12.5 %copy-start.3 = (bf16[1,2,128,128]{3,2,1,0:T(8,128)(2,1)S(1)}, bf16[1,2,128,128]{3,2,1,0:T(8,128)(2,1)}, u32[]{:S(2)}) copy-start(bf16[1,2,128,128]{3,2,1,0:T(8,128)(2,1)} %param.9) | copy-start | bytes 196612
  7.6 11.4 %copy-start.2 = (bf16[1,2,3,128,128]{4,3,2,1,0:T(8,128)(2,1)S(1)}, bf16[1,2,3,128,128]{4,3,2,1,0:T(8,128)(2,1)}, u32[]{:S(2)}) copy-start(bf16[1,2,3,128,128]{4,3,2,1,0:T(8,128)(2,1)} %param.7) | copy-start | bytes 589828
  7.6 32.5 %collective-permute-start = (bf16[248,128]{1,0:T(8,128)(2,1)S(1)}, bf16[248,128]{1,0:T(8,128)(2,1)S(1)}, u32[]{:S(2)}, u32[]{:S(2)}) collective-permute-start(bf16[248,128]{1,0:T(8,128)(2,1)S(1)} %get-tuple-element.15), channel_id=1, source_target_pairs={{0,4},{4,8},{8,12},{12,16},{16,20},{20,24},{24,28},{28,32},{32,36}... | collective-permute-start | bytes 190472 | tf_op jit(solution)/shard_map/ppermute | solution.py:11
  10.2 29.9 %collective-permute-start.1 = (bf16[248,128]{1,0:T(8,128)(2,1)S(1)}, bf16[248,128]{1,0:T(8,128)(2,1)S(1)}, u32[]{:S(2)}, u32[]{:S(2)}) collective-permute-start(bf16[248,128]{1,0:T(8,128)(2,1)S(1)} %get-tuple-element.16), channel_id=1, source_target_pairs={{0,252},{4,0},{8,4},{12,8},{16,12},{20,16},{24,20},{28,24},{32,28}... | collective-permute-start | bytes 190472 | tf_op jit(solution)/shard_map/ppermute | solution.py:11
  20.2 4.6 %copy-start.4 = (f32[1,2,128]{2,1,0:T(2,128)S(1)}, f32[1,2,128]{2,1,0:T(2,128)}, u32[]{:S(2)}) copy-start(f32[1,2,128]{2,1,0:T(2,128)} %param.8) | copy-start | bytes 3076
  20.3 4.6 %copy-start.5 = (f32[1,2,128]{2,1,0:T(2,128)S(1)}, f32[1,2,128]{2,1,0:T(2,128)}, u32[]{:S(2)}) copy-start(f32[1,2,128]{2,1,0:T(2,128)} %param.6) | copy-start | bytes 3076
  20.3 22.4 %all-to-all-start = ((bf16[4,1,8,128,128]{4,3,2,1,0:T(8,128)(2,1)}), bf16[4,1,8,128,128]{4,3,2,1,0:T(8,128)(2,1)S(1)}, u32[]{:S(2)}, u32[]{:S(2)}) async-start(bf16[4,1,8,128,128]{4,3,2,1,0:T(8,128)(2,1)} %stack.2), calls=%async_computation | async-start | bytes 2097152 | tf_op jit(solution)/shard_map/all_to_all | solution.py:74
  24.8 79.0 %all-gather.13.cloned.1.call-start = ((), (), s32[]{:S(2)}) async-start(), calls=%async_computation.3 | async-start | bytes 1310720 | tf_op jit(solution)/shard_map/all_gather | solution.py:102
  61.8 45.1 %all-gather.15.cloned.1.call-start = ((), (), s32[]{:S(2)}) async-start(), calls=%async_computation.4 | async-start | bytes 1310720 | tf_op jit(solution)/shard_map/all_gather | solution.py:102
  64.7 9.3 %collective-permute-start.2 = (bf16[256,128]{1,0:T(8,128)(2,1)S(1)}, bf16[256,128]{1,0:T(8,128)(2,1)S(1)}, u32[]{:S(2)}, u32[]{:S(2)}) collective-permute-start(bf16[256,128]{1,0:T(8,128)(2,1)S(1)} %get-tuple-element.14), channel_id=1, source_target_pairs={{0,4},{4,8},{8,12},{12,16},{16,20},{20,24},{24,28},{28,32},{32,36}... | collective-permute-start | bytes 196616 | tf_op jit(solution)/shard_map/ppermute | solution.py:11
  65.8 8.5 %collective-permute-start.3 = (bf16[256,128]{1,0:T(8,128)(2,1)S(1)}, bf16[256,128]{1,0:T(8,128)(2,1)S(1)}, u32[]{:S(2)}, u32[]{:S(2)}) collective-permute-start(bf16[256,128]{1,0:T(8,128)(2,1)S(1)} %get-tuple-element.13), channel_id=1, source_target_pairs={{0,252},{4,0},{8,4},{12,8},{16,12},{20,16},{24,20},{28,24},{32,28}... | collective-permute-start | bytes 196616 | tf_op jit(solution)/shard_map/ppermute | solution.py:11
  73.0 61.1 %all-gather.11.cloned.1.call-start = ((), (), s32[]{:S(2)}) async-start(), calls=%async_computation.2 | async-start | bytes 1310720 | tf_op jit(solution)/shard_map/all_gather | solution.py:102
  75.8 1.3 copy-start
  77.2 10.0 %collective-permute-start.4 = (bf16[512,128]{1,0:T(8,128)(2,1)S(1)}, bf16[512,128]{1,0:T(8,128)(2,1)S(1)}, u32[]{:S(2)}, u32[]{:S(2)}) collective-permute-start(bf16[512,128]{1,0:T(8,128)(2,1)S(1)} %get-tuple-element.9), channel_id=1, source_target_pairs={{0,4},{4,8},{8,12},{12,16},{16,20},{20,24},{24,28},{28,32},{32,36}... | collective-permute-start | bytes 393224 | tf_op jit(solution)/shard_map/ppermute | solution.py:11
  77.2 10.2 %collective-permute-start.5 = (bf16[512,128]{1,0:T(8,128)(2,1)S(1)}, bf16[512,128]{1,0:T(8,128)(2,1)S(1)}, u32[]{:S(2)}, u32[]{:S(2)}) collective-permute-start(bf16[512,128]{1,0:T(8,128)(2,1)S(1)} %get-tuple-element.10), channel_id=1, source_target_pairs={{0,252},{4,0},{8,4},{12,8},{16,12},{20,16},{24,20},{28,24},{32,28}... | collective-permute-start | bytes 393224 | tf_op jit(solution)/shard_map/ppermute | solution.py:11
  84.9 75.0 %all-gather.9.cloned.1.call-start = ((), (), s32[]{:S(2)}) async-start(), calls=%async_computation.1 | async-start | bytes 1310720 | tf_op jit(solution)/shard_map/all_gather | solution.py:102
  85.2 2.2 %copy-start.1 = (bf16[1024,128]{1,0:T(8,128)(2,1)S(1)}, bf16[1024,128]{1,0:T(8,128)(2,1)}, u32[]{:S(2)}) copy-start(bf16[1024,128]{1,0:T(8,128)(2,1)} %copy-done) | copy-start | bytes 786436
  90.2 11.1 %collective-permute-start.6 = (bf16[1024,128]{1,0:T(8,128)(2,1)S(1)}, bf16[1024,128]{1,0:T(8,128)(2,1)S(1)}, u32[]{:S(2)}, u32[]{:S(2)}) collective-permute-start(bf16[1024,128]{1,0:T(8,128)(2,1)S(1)} %fusion.205), channel_id=1, source_target_pairs={{0,4},{4,8},{8,12},{12,16},{16,20},{20,24},{24,28},{28,32},{32,36}... | collective-permute-start | bytes 786440 | tf_op jit(solution)/shard_map/ppermute | solution.py:11
  90.3 11.3 %collective-permute-start.7 = (bf16[1024,128]{1,0:T(8,128)(2,1)S(1)}, bf16[1024,128]{1,0:T(8,128)(2,1)S(1)}, u32[]{:S(2)}, u32[]{:S(2)}) collective-permute-start(bf16[1024,128]{1,0:T(8,128)(2,1)S(1)} %fusion.205), channel_id=1, source_target_pairs={{0,252},{4,0},{8,4},{12,8},{16,12},{20,16},{24,20},{28,24},{32,28}... | collective-permute-start | bytes 786440 | tf_op jit(solution)/shard_map/ppermute | solution.py:11
Sparse Core Ops, SparseCore 0:
  62.0 21.2 all-gather.12
  85.0 21.8 all-gather.14
  108.8 25.2 all-gather.10
  135.8 24.0 all-gather.8
